TPU v7x, 32 devices: a whole 2x2x4 slice. The times are simulated.
32 devices in a mesh: blk: 8 (over z, y), corpus: 4 (over x, core).
Axes of the slice: x: 2, y: 2, z: 4, core: 2. Of those that a mesh axis runs over, the one named last changes fastest.
Arguments:
- queries: bfloat16 [1024, 4096], P('blk', 'corpus'), may hold values from -12 to 12
- passages: bfloat16 [1024, 4096], P('blk', 'corpus'), may hold values from -4 to 4
- table: bfloat16 [1024, 4096], P('corpus'), may hold values from -4 to 4
- neg_owner: int32 [1024, 7], P('blk'), may hold values from 0 to 3, as said below
- neg_row: int32 [1024, 7], P('blk'), may hold values from 0 to 255
- positive: int32 [1024], P('blk'), may hold values from 0 to 1023, each once
- loss_weight: float32 [1024], P('blk'), may hold values from 32 to 256
Outputs:
- losses: float32 [1024], P(('blk', 'corpus'))
- query_grad: float32 [1024, 4096], P('blk', 'corpus')
- passage_grad: float32 [1024, 4096], P('blk', 'corpus')
- table_grad: float32 [1024, 4096], P('corpus', 'blk')
Inputs may be any that keep to these rules, and one draw needn't show every extreme that they name: `neg_owner`: among the 896 references of the queries of one index of blk (aligned blocks of 128 queries), one shard is named exactly 448 times and no shard more often.
All inputs are finite; a program needn't handle non-finite values.
Results may differ from a plain program's by a relative error of at most 0.0065.
Values may be sent and summed in bfloat16 or wider, within the bound.
No kernel may reach another device: no remote copies, remote signals or barrier semaphores. Data moves between devices by JAX's collectives and lax.ppermute only.
A program may use at most 128 MiB of HBM per device.

v0:
```python
import jax
import jax.numpy as jnp
from jax import lax
from jax.sharding import PartitionSpec as P


def hi_lo(mixing):
    upper = mixing.astype(jnp.bfloat16)
    lower = (mixing - upper.astype(jnp.float32)).astype(jnp.bfloat16)
    return (upper, lower)


def per_device(queries, passages, table, neg_owner, neg_row, positive, loss_weight):
    q_rows, col_width = queries.shape
    owner_count = lax.axis_size("corpus")
    blk_count = lax.axis_size("blk")
    factor = (col_width * owner_count) ** (-0.5)
    rows_shard = table.shape[0]
    table_rows = owner_count * rows_shard
    owner_index = lax.axis_index("corpus")
    blk_index = lax.axis_index("blk")
    table_cols = lax.all_to_all(table, "corpus", split_axis=1, concat_axis=0, tiled=True)
    all_passages = lax.all_gather(passages, "blk", axis=0, tiled=True)
    all_queries = lax.all_gather(queries, "blk", axis=0, tiled=True)
    ids = neg_owner * rows_shard + neg_row
    all_ids = lax.all_gather(ids, "blk", axis=0, tiled=True)
    all_rows = all_passages.shape[0]
    logits = lax.dot_general(
        queries, all_passages, (((1,), (1,)), ((), ())), preferred_element_type=jnp.float32
    )
    table_scores = lax.dot_general(
        queries, table_cols, (((1,), (1,)), ((), ())), preferred_element_type=jnp.float32
    )
    row_iota = jnp.arange(table_rows, dtype=jnp.int32)
    picks = ids[:, :, None] == row_iota[None, None, :]
    hard_logits = jnp.sum(jnp.where(picks, table_scores[:, None, :], 0.0), axis=2)
    logits, hard_logits = lax.psum((logits, hard_logits), "corpus")
    logits = logits * factor
    hard_logits = hard_logits * factor
    row_top = jnp.maximum(jnp.max(logits, axis=1), jnp.max(hard_logits, axis=1))
    log_total = row_top + jnp.log(
        jnp.sum(jnp.exp(logits - row_top[:, None]), axis=1)
        + jnp.sum(jnp.exp(hard_logits - row_top[:, None]), axis=1)
    )
    one_hot = positive[:, None] == jnp.arange(all_rows, dtype=jnp.int32)[None, :]
    losses = log_total - jnp.sum(jnp.where(one_hot, logits, 0.0), axis=1)
    share = q_rows // owner_count
    loss_share = lax.dynamic_slice_in_dim(losses, owner_index * share, share)
    weighting = (loss_weight * factor)[:, None]
    soft_grad = (
        weighting * (jnp.exp(logits - log_total[:, None]) - one_hot.astype(jnp.float32))
    ).astype(jnp.bfloat16)
    hard_grad = (weighting * jnp.exp(hard_logits - log_total[:, None])).astype(jnp.bfloat16)
    mixing = jnp.sum(jnp.where(picks, hard_grad.astype(jnp.float32)[:, :, None], 0.0), axis=1)
    mix_hi, mix_lo = hi_lo(mixing)
    left = jnp.concatenate([soft_grad, mix_hi, mix_lo], axis=1)
    right = jnp.concatenate([all_passages, table_cols, table_cols], axis=0)
    query_grad = jnp.dot(left, right, preferred_element_type=jnp.float32)
    soft_cols = lax.all_to_all(soft_grad, "blk", split_axis=1, concat_axis=0, tiled=True)
    passage_grad = lax.dot_general(
        soft_cols, all_queries, (((0,), (0,)), ((), ())), preferred_element_type=jnp.float32
    )
    all_hard = lax.all_gather(hard_grad, "blk", axis=0, tiled=True)
    per_col = blk_count // owner_count
    piece_width = col_width // per_col
    shard = blk_index // per_col
    part = blk_index % per_col
    shard_iota = shard * rows_shard + jnp.arange(rows_shard, dtype=jnp.int32)
    shard_picks = all_ids[:, :, None] == shard_iota[None, None, :]
    shard_mix = jnp.sum(
        jnp.where(shard_picks, all_hard.astype(jnp.float32)[:, :, None], 0.0), axis=1
    )
    shard_hi, shard_lo = hi_lo(shard_mix)
    query_part = lax.dynamic_slice_in_dim(all_queries, part * piece_width, piece_width, axis=1)
    dims = (((0,), (0,)), ((), ()))
    piece = lax.dot_general(
        shard_hi, query_part, dims, preferred_element_type=jnp.float32
    ) + lax.dot_general(shard_lo, query_part, dims, preferred_element_type=jnp.float32)
    perm = []
    for b in range(blk_count):
        for c in range(owner_count):
            dest_b = c * per_col + b % per_col
            dest_c = b // per_col
            perm.append((b * owner_count + c, dest_b * owner_count + dest_c))
    table_grad = lax.ppermute(piece, ("blk", "corpus"), perm)
    return (loss_share, query_grad, passage_grad, table_grad)


def solution(mesh):
    placed = (
        P("blk", "corpus"),
        P("blk", "corpus"),
        P("corpus", None),
        P("blk", None),
        P("blk", None),
        P("blk"),
        P("blk"),
    )
    return jax.shard_map(
        per_device,
        mesh=mesh,
        in_specs=placed,
        out_specs=(
            P(("blk", "corpus")),
            P("blk", "corpus"),
            P("blk", "corpus"),
            P("corpus", "blk"),
        ),
        check_vma=False,
    )
```

profile of v0, /device:TPU:2, one launch (start us, length us, event | category | flops | bytes accessed | tf_op | source)
XLA Modules:
  0.0 190.5 jit_solution(2006193391956256831)
XLA Ops:
  7.2 0.7 all-gather.3.cloned.1.call-update
  7.9 3.3 %copy.26 = bf16[256,4096]{0,1:T(8,128)(2,1)S(1)} copy(bf16[256,4096]{1,0:T(8,128)(2,1)} %param.9) | data formatting | bytes 4194304 | tf_op args[2]
  11.2 2.5 %copy.27 = bf16[256,4,1024]{2,0,1:T(8,128)(2,1)} copy(bf16[256,4,1024]{0,2,1:T(8,128)(2,1)S(1)} %bitcast.20) | data formatting | bytes 4194304 | tf_op jit(solution)/shard_map/all_to_all | solution.py:22
  13.7 3.7 %all-to-all-start = ((bf16[256,4,1024]{2,0,1:T(8,128)(2,1)}), bf16[256,4,1024]{2,0,1:T(8,128)(2,1)S(1)}, u32[]{:S(2)}, u32[]{:S(2)}) async-start(bf16[256,4,1024]{2,0,1:T(8,128)(2,1)} %copy.27), calls=%async_computation | async-start | bytes 4194304 | tf_op jit(solution)/shard_map/all_to_all | solution.py:22
  17.5 0.0 all-reduce.2.cloned.1.call-start
  17.5 42.9 %all-gather.3.cloned.1.call-done = bf16[1024,1024]{1,0:T(8,128)(2,1)} async-done(((bf16[128,1024]{1,0:T(8,128)(2,1)}), bf16[1024,1024]{1,0:T(8,128)(2,1)}) %all-gather.3.cloned.1.call-update) | async-done | bytes 2097168 | tf_op jit(solution)/shard_map/all_gather | solution.py:23
  60.5 3.2 %fusion.21 = f32[128,1024]{1,0:T(8,128)} fusion(bf16[128,1024]{1,0:T(8,128)(2,1)S(1)} %copy-done.2, bf16[1024,1024]{1,0:T(8,128)(2,1)} %all-gather.3.cloned.1.call-done), kind=kOutput, calls=%fused_computation.41 | convolution fusion | flops 268435456 | bytes 2883584 | tf_op jit(solution)/shard_map/dot_general | solution.py:28
  63.7 0.0 all-gather.5.cloned.1.call-start
  63.7 0.7 all-gather.5.cloned.1.call-update
  64.5 30.6 %all_gather.14 = s32[1024,7]{0,1:T(8,128)S(1)} all-gather(s32[128,7]{0,1:T(8,128)S(1)} %multiply_add_fusion), channel_id=1, replica_groups=mesh['blk'=8,'corpus'=4] {'blk'}, dimensions={0}, use_global_device_ids=true | all-gather | bytes 32256 | tf_op jit(solution)/shard_map/all_gather | solution.py:26
  95.1 0.8 fusion.22
  96.0 0.6 select_reduce_fusion.2
  96.6 5.9 %psum.15 = f32[128,7]{0,1:T(8,128)S(1)} all-reduce(f32[128,7]{0,1:T(8,128)S(1)} %select_reduce_fusion.2), channel_id=1, replica_groups=mesh['blk'=8,'corpus'=4] {'corpus'}, use_global_device_ids=true, to_apply=%region_3.4 | all-reduce | flops 896 | bytes 7168 | tf_op jit(solution)/shard_map/psum | solution.py:37
  102.5 1.2 multiply_reduce_fusion
  103.7 1.4 select_reduce_fusion.3
  105.1 2.1 %copy_bitcast_fusion = bf16[128,8,128]{2,0,1:T(8,128)(2,1)} fusion(s32[128]{0:T(128)S(1)} %copy-done.7, f32[128]{0:T(128)S(1)} %get-tuple-element.11, f32[128,1024]{1,0:T(8,128)} %all-reduce.2.cloned.1.call-done, f32[128]{0:T(128)S(1)} %broadcast_multiply_fusion), kind=kLoop, calls=%fused_computation.26 | loop fusion | flops 917504 | bytes 787968 | tf_op jit(solution)/shard_map/all_to_all | solution.py:59
  107.2 3.4 %all-to-all-start.1 = ((bf16[128,8,128]{2,0,1:T(8,128)(2,1)}), bf16[128,8,128]{2,0,1:T(8,128)(2,1)S(1)}, u32[]{:S(2)}, u32[]{:S(2)}) async-start(bf16[128,8,128]{2,0,1:T(8,128)(2,1)} %copy_bitcast_fusion), calls=%async_computation.1 | async-start | bytes 524288 | tf_op jit(solution)/shard_map/all_to_all | solution.py:59
  110.6 33.2 %all_gather.15 = bf16[1024,7]{0,1:T(8,128)(2,1)S(1)} all-gather(bf16[128,7]{0,1:T(8,128)(2,1)S(1)} %get-tuple-element.9), channel_id=1, replica_groups=mesh['blk'=8,'corpus'=4] {'blk'}, dimensions={0}, use_global_device_ids=true | all-gather | bytes 16128 | tf_op jit(solution)/shard_map/all_gather | solution.py:63
  143.8 0.5 select_reduce_fusion.1
  144.3 0.9 subtract_convert_fusion.2
  145.2 2.5 %select_reduce_fusion = f32[1024,256]{1,0:T(8,128)S(1)} fusion(f32[1024,7]{0,1:T(8,128)S(1)} %convert_element_type.40, s32[256]{0:T(256)S(1)} %iota_add_fusion, s32[1024,7]{0,1:T(8,128)S(1)} %all_gather.14), kind=kLoop, calls=%fused_computation | loop fusion | flops 5242880 | bytes 1106944 | tf_op jit(solution)/shard_map/reduce_sum | solution.py:70
  147.7 3.9 %all-gather.5.cloned.1.call-done = bf16[1024,1024]{1,0:T(8,128)(2,1)} async-done(((bf16[128,1024]{1,0:T(8,128)(2,1)}), bf16[1024,1024]{1,0:T(8,128)(2,1)}) %all-gather.5.cloned.1.call-update) | async-done | bytes 2097168 | tf_op jit(solution)/shard_map/all_gather | solution.py:24
  151.7 1.8 fusion.7
  153.5 0.1 copy-done
  153.6 1.3 convolution_add_fusion
  154.9 3.7 %collective-permute-start = (f32[256,512]{1,0:T(8,128)}, f32[256,512]{1,0:T(8,128)S(1)}, u32[]{:S(2)}, u32[]{:S(2)}) collective-permute-start(f32[256,512]{1,0:T(8,128)} %convolution_add_fusion), channel_id=1, source_target_pairs={{0,0},{1,8},{2,16},{3,24},{4,4},{5,12},{6,20},{7,28},{8,1},{9,9},{... | collective-permute-start | bytes 1572872 | tf_op jit(solution)/shard_map/ppermute | solution.py:85
  158.7 0.3 multiply_convert_fusion
  159.0 1.8 fusion
  160.8 0.6 dynamic_slice.6
  161.4 2.9 %fusion.23 = f32[128,1024]{1,0:T(8,128)} fusion(bf16[1024,128]{1,0:T(8,128)(2,1)S(1)} %bitcast.21, bf16[1024,1024]{1,0:T(8,128)(2,1)} %all-gather.5.cloned.1.call-done), kind=kOutput, calls=%fused_computation.43 | convolution fusion | flops 268435456 | bytes 2883584 | tf_op jit(solution)/shard_map/dot_general | solution.py:60
  164.2 19.0 %collective-permute-done = f32[256,512]{1,0:T(8,128)S(1)} collective-permute-done((f32[256,512]{1,0:T(8,128)}, f32[256,512]{1,0:T(8,128)S(1)}, u32[]{:S(2)}, u32[]{:S(2)}) %collective-permute-start) | collective-permute-done | bytes 524320 | tf_op jit(solution)/shard_map/ppermute | solution.py:85
  183.2 0.8 copy.33
  (35 shorter events, 0.2 us)
Async XLA Ops:
  7.2 53.3 %all-gather.3.cloned.1.call-start = ((), (), s32[]{:S(2)}) async-start(), calls=%async_computation.2 | async-start | bytes 2359296 | tf_op jit(solution)/shard_map/all_gather | solution.py:23
  13.7 46.8 %copy-start.2 = (bf16[128,1024]{1,0:T(8,128)(2,1)S(1)}, bf16[128,1024]{1,0:T(8,128)(2,1)}, u32[]{:S(2)}) copy-start(bf16[128,1024]{1,0:T(8,128)(2,1)} %param.7) | copy-start | bytes 786436
  13.7 81.4 %all-to-all-start = ((bf16[256,4,1024]{2,0,1:T(8,128)(2,1)}), bf16[256,4,1024]{2,0,1:T(8,128)(2,1)S(1)}, u32[]{:S(2)}, u32[]{:S(2)}) async-start(bf16[256,4,1024]{2,0,1:T(8,128)(2,1)} %copy.27), calls=%async_computation | async-start | bytes 4194304 | tf_op jit(solution)/shard_map/all_to_all | solution.py:22
  17.4 47.0 %copy-start.8 = (s32[128,7]{0,1:T(8,128)S(1)}, s32[128,7]{0,1:T(8,128)}, u32[]{:S(2)}) copy-start(s32[128,7]{0,1:T(8,128)} %param.11) | copy-start | bytes 10756
  17.4 47.0 %copy-start.9 = (s32[128,7]{0,1:T(8,128)S(1)}, s32[128,7]{0,1:T(8,128)}, u32[]{:S(2)}) copy-start(s32[128,7]{0,1:T(8,128)} %param.10) | copy-start | bytes 10756
  17.5 77.7 %copy-start.10 = (f32[128]{0:T(128)S(1)}, f32[128]{0:T(128)}, u32[]{:S(2)}) copy-start(f32[128]{0:T(128)} %param.13) | copy-start | bytes 1540
  17.5 77.7 %copy-start.3 = (bf16[128,1024]{1,0:T(8,128)(2,1)S(1)}, bf16[128,1024]{1,0:T(8,128)(2,1)}, u32[]{:S(2)}) copy-start(bf16[128,1024]{1,0:T(8,128)(2,1)} %param.7) | copy-start | bytes 786436
  17.5 85.1 %all-reduce.2.cloned.1.call-start = ((), (), s32[]{:S(2)}) async-start(), calls=%async_computation.3 | async-start | bytes 1048576 | tf_op jit(solution)/shard_map/psum | solution.py:37
  63.7 88.0 %all-gather.5.cloned.1.call-start = ((), (), s32[]{:S(2)}) async-start(), calls=%async_computation.4 | async-start | bytes 2359296 | tf_op jit(solution)/shard_map/all_gather | solution.py:24
  64.4 39.3 %copy-start.7 = (s32[128]{0:T(128)S(1)}, s32[128]{0:T(128)}, u32[]{:S(2)}) copy-start(s32[128]{0:T(128)} %param.12) | copy-start | bytes 1540
  107.2 54.2 %all-to-all-start.1 = ((bf16[128,8,128]{2,0,1:T(8,128)(2,1)}), bf16[128,8,128]{2,0,1:T(8,128)(2,1)S(1)}, u32[]{:S(2)}, u32[]{:S(2)}) async-start(bf16[128,8,128]{2,0,1:T(8,128)(2,1)} %copy_bitcast_fusion), calls=%async_computation.1 | async-start | bytes 524288 | tf_op jit(solution)/shard_map/all_to_all | solution.py:59
  151.7 1.9 %copy-start = (bf16[1024,1024]{1,0:T(8,128)(2,1)S(1)}, bf16[1024,1024]{1,0:T(8,128)(2,1)}, u32[]{:S(2)}) copy-start(bf16[1024,1024]{1,0:T(8,128)(2,1)} %all-gather.5.cloned.1.call-done) | copy-start | bytes 6291460
  153.6 5.0 %copy-start.1 = (f32[128,1024]{1,0:T(8,128)S(1)}, f32[128,1024]{1,0:T(8,128)}, u32[]{:S(2)}) copy-start(f32[128,1024]{1,0:T(8,128)} %all-reduce.2.cloned.1.call-done) | copy-start | bytes 1572868
  153.6 5.3 %copy-start.4 = (bf16[1024,1024]{1,0:T(8,128)(2,1)S(1)}, bf16[1024,1024]{1,0:T(8,128)(2,1)}, u32[]{:S(2)}) copy-start(bf16[1024,1024]{1,0:T(8,128)(2,1)} %all-gather.3.cloned.1.call-done) | copy-start | bytes 6291460
  153.6 5.3 %copy-start.5 = (bf16[128,1024]{1,0:T(8,128)(2,1)S(1)}, bf16[128,1024]{1,0:T(8,128)(2,1)}, u32[]{:S(2)}) copy-start(bf16[128,1024]{1,0:T(8,128)(2,1)} %get-tuple-element.6) | copy-start | bytes 786436
  153.6 5.4 %copy-start.6 = (bf16[128,1024]{1,0:T(8,128)(2,1)S(1)}, bf16[128,1024]{1,0:T(8,128)(2,1)}, u32[]{:S(2)}) copy-start(bf16[128,1024]{1,0:T(8,128)(2,1)} %get-tuple-element.7) | copy-start | bytes 786436
  154.9 28.3 %collective-permute-start = (f32[256,512]{1,0:T(8,128)}, f32[256,512]{1,0:T(8,128)S(1)}, u32[]{:S(2)}, u32[]{:S(2)}) collective-permute-start(f32[256,512]{1,0:T(8,128)} %convolution_add_fusion), channel_id=1, source_target_pairs={{0,0},{1,8},{2,16},{3,24},{4,4},{5,12},{6,20},{7,28},{8,1},{9,9},{... | collective-permute-start | bytes 1572872 | tf_op jit(solution)/shard_map/ppermute | solution.py:85
Sparse Core Ops, SparseCore 0:
  10.1 50.3 all-gather.2
  63.8 30.5 all-reduce.1
  96.6 55.0 all-gather.4
where the time goes:
time: 191 us
  blocking collectives  69.8 us (37%)
  waiting for transfers between devices  67.3 us (35%)
  between operations  14 us (7%)
  matrix products  11.8 us (6%)
  starting transfers between devices  11 us (6%)
  other arithmetic  9.43 us (5%)
  local copies, waits for them, and re-layouts  7.28 us (4%)
    all_gather x1, waiting for transfers between devices, per_device(): all_passages = lax.all_gather(passages, 'blk', axis=0, tiled=True)  42.9 us
    all_gather x1, blocking collectives, per_device(): all_hard = lax.all_gather(hard_grad, 'blk', axis=0, tiled=True)  33.2 us
    all_gather x1, blocking collectives, per_device(): all_ids = lax.all_gather(ids, 'blk', axis=0, tiled=True)  30.6 us
    ppermute x1, waiting for transfers between devices, per_device(): table_grad = lax.ppermute(piece, ('blk', 'corpus'), perm)  19 us
    psum x1, blocking collectives, per_device(): logits, hard_logits = lax.psum((logits, hard_logits), 'corpus')  5.93 us
    unnamed x24, local copies, waits for them, and re-layouts  4.18 us
    all_gather x1, waiting for transfers between devices, per_device(): all_queries = lax.all_gather(queries, 'blk', axis=0, tiled=True)  3.95 us
  transfers between devices with their start and end apart: 6, of which 3 were waited for; matrix products, arithmetic and copies ran while one was open for 14% of the time, Pallas kernels for 0%

commit v1 on v0

--- a/solution.py
+++ b/solution.py
@@ -2,6 +2,27 @@
 import jax.numpy as jnp
 from jax import lax
 from jax.sharding import PartitionSpec as P
+
+
+def collect(shard, axis, dim):
+    length, position, rows = (lax.axis_size(axis), lax.axis_index(axis), shard.shape[dim])
+    forward = [(i, (i + 1) % length) for i in range(length)]
+    left = [(i, (i - 1) % length) for i in range(length)]
+    whole = jnp.zeros((*shard.shape[:dim], length * rows, *shard.shape[dim + 1 :]), shard.dtype)
+    whole = lax.dynamic_update_slice_in_dim(whole, shard, position * rows, axis=dim)
+    from_left = from_right = shard
+    half = length // 2
+    for hop in range(1, half + 1):
+        from_left = lax.ppermute(from_left, axis, forward)
+        whole = lax.dynamic_update_slice_in_dim(
+            whole, from_left, (position - hop) % length * rows, axis=dim
+        )
+        if hop < length - half:
+            from_right = lax.ppermute(from_right, axis, left)
+            whole = lax.dynamic_update_slice_in_dim(
+                whole, from_right, (position + hop) % length * rows, axis=dim
+            )
+    return whole
 
 
 def hi_lo(mixing):
@@ -20,7 +41,7 @@
     owner_index = lax.axis_index("corpus")
     blk_index = lax.axis_index("blk")
     table_cols = lax.all_to_all(table, "corpus", split_axis=1, concat_axis=0, tiled=True)
-    all_passages = lax.all_gather(passages, "blk", axis=0, tiled=True)
+    all_passages = collect(passages, "blk", 0)
     all_queries = lax.all_gather(queries, "blk", axis=0, tiled=True)
     ids = neg_owner * rows_shard + neg_row
     all_ids = lax.all_gather(ids, "blk", axis=0, tiled=True)

time: 191 us -> 185 us (0.969)
  waiting for transfers between devices: 67.3 us -> 45.8 us
  starting transfers between devices: 11 us -> 28.5 us
  blocking collectives: 69.8 us -> 65.2 us
  other arithmetic: 9.43 us -> 6.11 us
  local copies, waits for them, and re-layouts: 7.28 us -> 10.5 us
    all_gather x1 -> x0, waiting for transfers between devices: 42.9 us -> none  [per_device(): all_passages = lax.all_gather(passages, 'blk', axis=0, tiled=True)]
    ppermute x0 -> x7, waiting for transfers between devices: none -> 30.3 us  [the longest x4 30.3 us: collect(): from_left = lax.ppermute(from_left, axis, forward)]
    ppermute x0 -> x7, starting transfers between devices: none -> 18.2 us  [the longest x3 9.34 us: collect(): from_right = lax.ppermute(from_right, axis, left)]
    all_gather x1, blocking collectives: 33.2 us -> 28.3 us  [per_device(): all_hard = lax.all_gather(hard_grad, 'blk', axis=0, tiled=True)]
    ppermute x1, waiting for transfers between devices: 19 us -> 14.8 us  [per_device(): table_grad = lax.ppermute(piece, ('blk', 'corpus'), perm)]
    all_gather x1, waiting for transfers between devices: 3.95 us -> 0.03 us  [per_device(): all_queries = lax.all_gather(queries, 'blk', axis=0, tiled=True)]
    all_to_all x1 -> x0, other arithmetic: 2.05 us -> none  [per_device(): lax.all_to_all(soft_grad, 'blk', split_axis=1, concat_axis=0, tiled=True)]
    unnamed x24 -> x28, local copies, waits for them, and re-layouts: 4.18 us -> 4.97 us
  transfers between devices with their start and end apart: 6 -> 12, of which waited for: 3 -> 5; matrix products, arithmetic and copies ran while one was open for 14% -> 15% of each run, Pallas kernels for 0% -> 0%
where the time goes in v1:
time: 185 us
  blocking collectives  65.2 us (35%)
  waiting for transfers between devices  45.8 us (25%)
  starting transfers between devices  28.5 us (15%)
  between operations  15.9 us (9%)
  matrix products  12.7 us (7%)
  local copies, waits for them, and re-layouts  10.5 us (6%)
  other arithmetic  6.11 us (3%)
    all_gather x1, blocking collectives, per_device(): all_ids = lax.all_gather(ids, 'blk', axis=0, tiled=True)  30.8 us
    ppermute x4, waiting for transfers between devices, collect(): from_left = lax.ppermute(from_left, axis, forward)  30.3 us
    all_gather x1, blocking collectives, per_device(): all_hard = lax.all_gather(hard_grad, 'blk', axis=0, tiled=True)  28.3 us
    ppermute x1, waiting for transfers between devices, per_device(): table_grad = lax.ppermute(piece, ('blk', 'corpus'), perm)  14.8 us
    ppermute x3, starting transfers between devices, collect(): from_right = lax.ppermute(from_right, axis, left)  9.34 us
    ppermute x4, starting transfers between devices, collect(): from_left = lax.ppermute(from_left, axis, forward)  8.91 us
    psum x1, blocking collectives, per_device(): logits, hard_logits = lax.psum((logits, hard_logits), 'corpus')  6.08 us
    unnamed x28, local copies, waits for them, and re-layouts  4.97 us
  transfers between devices with their start and end apart: 12, of which 5 were waited for; matrix products, arithmetic and copies ran while one was open for 15% of the time, Pallas kernels for 0%

profile of v1, /device:TPU:2, one launch (start us, length us, event | category | flops | bytes accessed | tf_op | source)
XLA Modules:
  0.0 184.8 jit_solution(17547856445293310696)
XLA Ops:
  8.1 1.6 collective-permute-start
  9.6 3.2 %collective-permute-start.1 = (bf16[128,1024]{1,0:T(8,128)(2,1)}, bf16[128,1024]{1,0:T(8,128)(2,1)S(1)}, u32[]{:S(2)}, u32[]{:S(2)}) collective-permute-start(bf16[128,1024]{1,0:T(8,128)(2,1)} %param.8), channel_id=1, source_target_pairs={{0,28},{4,0},{8,4},{12,8},{16,12},{20,16},{24,20},{28,24},{1,29},{... | collective-permute-start | bytes 786440 | tf_op jit(solution)/shard_map/ppermute | solution.py:21
  12.8 8.3 %collective-permute-done = bf16[128,1024]{1,0:T(8,128)(2,1)S(1)} collective-permute-done((bf16[128,1024]{1,0:T(8,128)(2,1)}, bf16[128,1024]{1,0:T(8,128)(2,1)S(1)}, u32[]{:S(2)}, u32[]{:S(2)}) %collective-permute-start) | collective-permute-done | bytes 262176 | tf_op jit(solution)/shard_map/ppermute | solution.py:16
  21.1 2.4 %collective-permute-start.2 = (bf16[128,1024]{1,0:T(8,128)(2,1)S(1)}, bf16[128,1024]{1,0:T(8,128)(2,1)S(1)}, u32[]{:S(2)}, u32[]{:S(2)}) collective-permute-start(bf16[128,1024]{1,0:T(8,128)(2,1)S(1)} %collective-permute-done), channel_id=1, source_target_pairs={{0,4},{4,8},{8,12},{12,16},{16,20},{20,24},{24,28},{28,0},{1,5},{5... | collective-permute-start | bytes 786440 | tf_op jit(solution)/shard_map/ppermute | solution.py:16
  23.5 3.0 %collective-permute-start.3 = (bf16[128,1024]{1,0:T(8,128)(2,1)S(1)}, bf16[128,1024]{1,0:T(8,128)(2,1)}, u32[]{:S(2)}, u32[]{:S(2)}) collective-permute-start(bf16[128,1024]{1,0:T(8,128)(2,1)S(1)} %collective-permute-done.1), channel_id=1, source_target_pairs={{0,28},{4,0},{8,4},{12,8},{16,12},{20,16},{24,20},{28,24},{1,29},{... | collective-permute-start | bytes 786440 | tf_op jit(solution)/shard_map/ppermute | solution.py:21
  27.0 6.8 %collective-permute-done.2 = bf16[128,1024]{1,0:T(8,128)(2,1)S(1)} collective-permute-done((bf16[128,1024]{1,0:T(8,128)(2,1)S(1)}, bf16[128,1024]{1,0:T(8,128)(2,1)S(1)}, u32[]{:S(2)}, u32[]{:S(2)}) %collective-permute-start.2) | collective-permute-done | bytes 262176 | tf_op jit(solution)/shard_map/ppermute | solution.py:16
  33.8 2.5 %collective-permute-start.4 = (bf16[128,1024]{1,0:T(8,128)(2,1)S(1)}, bf16[128,1024]{1,0:T(8,128)(2,1)S(1)}, u32[]{:S(2)}, u32[]{:S(2)}) collective-permute-start(bf16[128,1024]{1,0:T(8,128)(2,1)S(1)} %collective-permute-done.2), channel_id=1, source_target_pairs={{0,4},{4,8},{8,12},{12,16},{16,20},{20,24},{24,28},{28,0},{1,5},{5... | collective-permute-start | bytes 786440 | tf_op jit(solution)/shard_map/ppermute | solution.py:16
  36.4 3.1 %collective-permute-start.5 = (bf16[128,1024]{1,0:T(8,128)(2,1)}, bf16[128,1024]{1,0:T(8,128)(2,1)S(1)}, u32[]{:S(2)}, u32[]{:S(2)}) collective-permute-start(bf16[128,1024]{1,0:T(8,128)(2,1)} %collective-permute-done.3), channel_id=1, source_target_pairs={{0,28},{4,0},{8,4},{12,8},{16,12},{20,16},{24,20},{28,24},{1,29},{... | collective-permute-start | bytes 786440 | tf_op jit(solution)/shard_map/ppermute | solution.py:21
  39.5 6.5 %collective-permute-done.4 = bf16[128,1024]{1,0:T(8,128)(2,1)S(1)} collective-permute-done((bf16[128,1024]{1,0:T(8,128)(2,1)S(1)}, bf16[128,1024]{1,0:T(8,128)(2,1)S(1)}, u32[]{:S(2)}, u32[]{:S(2)}) %collective-permute-start.4) | collective-permute-done | bytes 262176 | tf_op jit(solution)/shard_map/ppermute | solution.py:16
  46.0 2.5 %collective-permute-start.6 = (bf16[128,1024]{1,0:T(8,128)(2,1)S(1)}, bf16[128,1024]{1,0:T(8,128)(2,1)S(1)}, u32[]{:S(2)}, u32[]{:S(2)}) collective-permute-start(bf16[128,1024]{1,0:T(8,128)(2,1)S(1)} %collective-permute-done.4), channel_id=1, source_target_pairs={{0,4},{4,8},{8,12},{12,16},{16,20},{20,24},{24,28},{28,0},{1,5},{5... | collective-permute-start | bytes 786440 | tf_op jit(solution)/shard_map/ppermute | solution.py:16
  48.4 1.0 constant_dynamic-update-slice_fusion.3
  49.5 8.7 %collective-permute-done.6 = bf16[128,1024]{1,0:T(8,128)(2,1)S(1)} collective-permute-done((bf16[128,1024]{1,0:T(8,128)(2,1)S(1)}, bf16[128,1024]{1,0:T(8,128)(2,1)S(1)}, u32[]{:S(2)}, u32[]{:S(2)}) %collective-permute-start.6) | collective-permute-done | bytes 262176 | tf_op jit(solution)/shard_map/ppermute | solution.py:16
  58.3 1.5 convolution_bitcast_fusion
  59.8 4.1 %copy.21 = bf16[256,4096]{0,1:T(8,128)(2,1)} copy(bf16[256,4096]{1,0:T(8,128)(2,1)} %param.9) | data formatting | bytes 4194304 | tf_op args[2]
  63.9 4.3 %all-to-all-start = ((bf16[256,4,1024]{0,2,1:T(8,128)(2,1)}), bf16[256,4,1024]{0,2,1:T(8,128)(2,1)S(1)}, u32[]{:S(2)}, u32[]{:S(2)}) async-start(bf16[256,4,1024]{0,2,1:T(8,128)(2,1)} %bitcast.16), calls=%async_computation | async-start | bytes 4194304 | tf_op jit(solution)/shard_map/all_to_all | solution.py:43
  68.8 30.8 %all_gather.10 = s32[1024,7]{0,1:T(8,128)S(1)} all-gather(s32[128,7]{0,1:T(8,128)S(1)} %multiply_add_fusion), channel_id=1, replica_groups=mesh['blk'=8,'corpus'=4] {'blk'}, dimensions={0}, use_global_device_ids=true | all-gather | bytes 32256 | tf_op jit(solution)/shard_map/all_gather | solution.py:47
  99.6 1.2 multiply_reduce_fusion
  100.9 2.5 %copy.22 = bf16[4,256,1024]{2,1,0:T(8,128)(2,1)} copy(bf16[4,256,1024]{1,2,0:T(8,128)(2,1)S(1)} %bitcast.15) | data formatting | bytes 4194304 | tf_op jit(solution)/shard_map/all_to_all | solution.py:43
  103.4 2.5 %fusion.21 = f32[128,1024]{1,0:T(8,128)S(1)} fusion(bf16[128,1024]{1,0:T(8,128)(2,1)S(1)} %copy-done.5, bf16[1024,1024]{1,0:T(8,128)(2,1)} %bitcast.17), kind=kOutput, calls=%fused_computation.49 | convolution fusion | flops 268435456 | bytes 2883584 | tf_op jit(solution)/shard_map/dot_general | solution.py:52
  106.5 6.1 %psum.15 = f32[128,7]{0,1:T(8,128)S(1)} all-reduce(f32[128,7]{0,1:T(8,128)S(1)} %select_reduce_fusion.2), channel_id=1, replica_groups=mesh['blk'=8,'corpus'=4] {'corpus'}, use_global_device_ids=true, to_apply=%region_3.4 | all-reduce | flops 896 | bytes 7168 | tf_op jit(solution)/shard_map/psum | solution.py:58
  113.7 0.9 copy.25
  114.6 4.0 %all-to-all-start.1 = ((bf16[128,8,128]{2,0,1:T(8,128)(2,1)}), bf16[128,8,128]{2,0,1:T(8,128)(2,1)}, u32[]{:S(2)}, u32[]{:S(2)}) async-start(bf16[128,8,128]{2,0,1:T(8,128)(2,1)} %copy.25), calls=%async_computation.1 | async-start | bytes 524288 | tf_op jit(solution)/shard_map/all_to_all | solution.py:80
  118.6 28.3 %all_gather.11 = bf16[1024,7]{0,1:T(8,128)(2,1)S(1)} all-gather(bf16[128,7]{0,1:T(8,128)(2,1)S(1)} %get-tuple-element.9), channel_id=1, replica_groups=mesh['blk'=8,'corpus'=4] {'blk'}, dimensions={0}, use_global_device_ids=true | all-gather | bytes 16128 | tf_op jit(solution)/shard_map/all_gather | solution.py:84
  146.9 0.9 subtract_convert_fusion.2
  147.8 2.5 %select_reduce_fusion = f32[1024,256]{1,0:T(8,128)S(1)} fusion(f32[1024,7]{0,1:T(8,128)S(1)} %convert_element_type.40, s32[256]{0:T(256)S(1)} %iota_add_fusion, s32[1024,7]{0,1:T(8,128)S(1)} %all_gather.10), kind=kLoop, calls=%fused_computation | loop fusion | flops 5242880 | bytes 1106944 | tf_op jit(solution)/shard_map/reduce_sum | solution.py:91
  150.4 1.8 fusion.7
  152.3 1.3 convolution_add_fusion
  153.6 1.9 %collective-permute-start.7 = (f32[256,512]{1,0:T(8,128)}, f32[256,512]{1,0:T(8,128)S(1)}, u32[]{:S(2)}, u32[]{:S(2)}) collective-permute-start(f32[256,512]{1,0:T(8,128)} %convolution_add_fusion), channel_id=1, source_target_pairs={{0,0},{1,8},{2,16},{3,24},{4,4},{5,12},{6,20},{7,28},{8,1},{9,9},{... | collective-permute-start | bytes 1572872 | tf_op jit(solution)/shard_map/ppermute | solution.py:106
  155.5 3.4 %fusion = f32[128,1024]{1,0:T(8,128)} fusion(bf16[1024,1024]{1,0:T(8,128)(2,1)S(1)} %bitcast.18, bf16[1024,1024]{1,0:T(8,128)(2,1)} %copy-done.2, bf16[128,1024]{0,1:T(8,128)(2,1)S(1)} %copy-done.7, bf16[128,1024]{0,1:T(8,128)(2,1)S(1)} %copy-done.8, bf16[128,1024]{0,1:T(8,128)(2,1)S(1)} %multiply_convert_fusion), kind=kOutput, calls=%fused_computation.1 | convolution fusion | flops 826540032 | bytes 5505024 | tf_op jit(solution)/shard_map/dot_general | solution.py:79
  159.5 2.2 %fusion.22 = f32[128,1024]{1,0:T(8,128)} fusion(bf16[1024,128]{1,0:T(8,128)(2,1)} %bitcast.6, bf16[1024,1024]{1,0:T(8,128)(2,1)S(1)} %copy-done), kind=kOutput, calls=%fused_computation.50 | convolution fusion | flops 268435456 | bytes 2883584 | tf_op jit(solution)/shard_map/dot_general | solution.py:81
  161.7 14.8 %collective-permute-done.7 = f32[256,512]{1,0:T(8,128)S(1)} collective-permute-done((f32[256,512]{1,0:T(8,128)}, f32[256,512]{1,0:T(8,128)S(1)}, u32[]{:S(2)}, u32[]{:S(2)}) %collective-permute-start.7) | collective-permute-done | bytes 524320 | tf_op jit(solution)/shard_map/ppermute | solution.py:106
  176.5 0.8 copy.36
  (60 shorter events, 3.5 us)
Async XLA Ops:
  8.0 18.8 %copy-start.6 = (bf16[128,1024]{1,0:T(8,128)(2,1)S(1)}, bf16[128,1024]{1,0:T(8,128)(2,1)}, u32[]{:S(2)}) copy-start(bf16[128,1024]{1,0:T(8,128)(2,1)} %param.8) | copy-start | bytes 786436
  8.0 91.6 %all-reduce.2.cloned.1.call-start = ((), (), s32[]{:S(2)}) async-start(), calls=%async_computation.2 | async-start | bytes 1048576 | tf_op jit(solution)/shard_map/psum | solution.py:58
  8.1 13.1 %collective-permute-start = (bf16[128,1024]{1,0:T(8,128)(2,1)}, bf16[128,1024]{1,0:T(8,128)(2,1)S(1)}, u32[]{:S(2)}, u32[]{:S(2)}) collective-permute-start(bf16[128,1024]{1,0:T(8,128)(2,1)} %param.8), channel_id=1, source_target_pairs={{0,4},{4,8},{8,12},{12,16},{16,20},{20,24},{24,28},{28,0},{1,5},{5... | collective-permute-start | bytes 786440 | tf_op jit(solution)/shard_map/ppermute | solution.py:16
  9.6 13.9 %collective-permute-start.1 = (bf16[128,1024]{1,0:T(8,128)(2,1)}, bf16[128,1024]{1,0:T(8,128)(2,1)S(1)}, u32[]{:S(2)}, u32[]{:S(2)}) collective-permute-start(bf16[128,1024]{1,0:T(8,128)(2,1)} %param.8), channel_id=1, source_target_pairs={{0,28},{4,0},{8,4},{12,8},{16,12},{20,16},{24,20},{28,24},{1,29},{... | collective-permute-start | bytes 786440 | tf_op jit(solution)/shard_map/ppermute | solution.py:21
  21.1 12.7 %collective-permute-start.2 = (bf16[128,1024]{1,0:T(8,128)(2,1)S(1)}, bf16[128,1024]{1,0:T(8,128)(2,1)S(1)}, u32[]{:S(2)}, u32[]{:S(2)}) collective-permute-start(bf16[128,1024]{1,0:T(8,128)(2,1)S(1)} %collective-permute-done), channel_id=1, source_target_pairs={{0,4},{4,8},{8,12},{12,16},{16,20},{20,24},{24,28},{28,0},{1,5},{5... | collective-permute-start | bytes 786440 | tf_op jit(solution)/shard_map/ppermute | solution.py:16
  23.5 12.9 %collective-permute-start.3 = (bf16[128,1024]{1,0:T(8,128)(2,1)S(1)}, bf16[128,1024]{1,0:T(8,128)(2,1)}, u32[]{:S(2)}, u32[]{:S(2)}) collective-permute-start(bf16[128,1024]{1,0:T(8,128)(2,1)S(1)} %collective-permute-done.1), channel_id=1, source_target_pairs={{0,28},{4,0},{8,4},{12,8},{16,12},{20,16},{24,20},{28,24},{1,29},{... | collective-permute-start | bytes 786440 | tf_op jit(solution)/shard_map/ppermute | solution.py:21
  26.8 31.4 %copy-start.4 = (bf16[128,1024]{1,0:T(8,128)(2,1)S(1)}, bf16[128,1024]{1,0:T(8,128)(2,1)}, u32[]{:S(2)}) copy-start(bf16[128,1024]{1,0:T(8,128)(2,1)} %param.7) | copy-start | bytes 786436
  33.8 12.1 %collective-permute-start.4 = (bf16[128,1024]{1,0:T(8,128)(2,1)S(1)}, bf16[128,1024]{1,0:T(8,128)(2,1)S(1)}, u32[]{:S(2)}, u32[]{:S(2)}) collective-permute-start(bf16[128,1024]{1,0:T(8,128)(2,1)S(1)} %collective-permute-done.2), channel_id=1, source_target_pairs={{0,4},{4,8},{8,12},{12,16},{16,20},{20,24},{24,28},{28,0},{1,5},{5... | collective-permute-start | bytes 786440 | tf_op jit(solution)/shard_map/ppermute | solution.py:16
  36.4 13.1 %collective-permute-start.5 = (bf16[128,1024]{1,0:T(8,128)(2,1)}, bf16[128,1024]{1,0:T(8,128)(2,1)S(1)}, u32[]{:S(2)}, u32[]{:S(2)}) collective-permute-start(bf16[128,1024]{1,0:T(8,128)(2,1)} %collective-permute-done.3), channel_id=1, source_target_pairs={{0,28},{4,0},{8,4},{12,8},{16,12},{20,16},{24,20},{28,24},{1,29},{... | collective-permute-start | bytes 786440 | tf_op jit(solution)/shard_map/ppermute | solution.py:21
  46.0 12.2 %collective-permute-start.6 = (bf16[128,1024]{1,0:T(8,128)(2,1)S(1)}, bf16[128,1024]{1,0:T(8,128)(2,1)S(1)}, u32[]{:S(2)}, u32[]{:S(2)}) collective-permute-start(bf16[128,1024]{1,0:T(8,128)(2,1)S(1)} %collective-permute-done.4), channel_id=1, source_target_pairs={{0,4},{4,8},{8,12},{12,16},{16,20},{20,24},{24,28},{28,0},{1,5},{5... | collective-permute-start | bytes 786440 | tf_op jit(solution)/shard_map/ppermute | solution.py:16
  58.2 5.6 %copy-start.2 = (bf16[1024,1024]{1,0:T(8,128)(2,1)}, bf16[1024,1024]{1,0:T(8,128)(2,1)S(1)}, u32[]{:S(2)}) copy-start(bf16[1024,1024]{1,0:T(8,128)(2,1)S(1)} %constant_dynamic-update-slice_fusion) | copy-start | bytes 6291460
  63.9 4.9 %copy-start.9 = (s32[128,7]{0,1:T(8,128)S(1)}, s32[128,7]{0,1:T(8,128)}, u32[]{:S(2)}) copy-start(s32[128,7]{0,1:T(8,128)} %param.11) | copy-start | bytes 10756
  63.9 4.9 %copy-start.10 = (s32[128,7]{0,1:T(8,128)S(1)}, s32[128,7]{0,1:T(8,128)}, u32[]{:S(2)}) copy-start(s32[128,7]{0,1:T(8,128)} %param.10) | copy-start | bytes 10756
  63.9 35.7 %copy-start.12 = (f32[128]{0:T(128)S(1)}, f32[128]{0:T(128)}, u32[]{:S(2)}) copy-start(f32[128]{0:T(128)} %param.13) | copy-start | bytes 1540
  63.9 36.9 %all-to-all-start = ((bf16[256,4,1024]{0,2,1:T(8,128)(2,1)}), bf16[256,4,1024]{0,2,1:T(8,128)(2,1)S(1)}, u32[]{:S(2)}, u32[]{:S(2)}) async-start(bf16[256,4,1024]{0,2,1:T(8,128)(2,1)} %bitcast.16), calls=%async_computation | async-start | bytes 4194304 | tf_op jit(solution)/shard_map/all_to_all | solution.py:43
  68.2 82.2 %all-gather.2.cloned.1.call-start = ((), (), s32[]{:S(2)}) async-start(), calls=%async_computation.3 | async-start | bytes 2359296 | tf_op jit(solution)/shard_map/all_gather | solution.py:45
  100.8 2.6 %copy-start.5 = (bf16[128,1024]{1,0:T(8,128)(2,1)S(1)}, bf16[128,1024]{1,0:T(8,128)(2,1)}, u32[]{:S(2)}) copy-start(bf16[128,1024]{1,0:T(8,128)(2,1)} %param.7) | copy-start | bytes 786436
  103.4 9.2 %copy-start.3 = (f32[128,1024]{0,1:T(8,128)S(1)}, f32[128,1024]{0,1:T(8,128)}, u32[]{:S(2)}) copy-start(f32[128,1024]{0,1:T(8,128)} %all-reduce.2.cloned.1.call-done) | copy-start | bytes 1572868
  103.4 9.2 %copy-start.11 = (s32[128]{0:T(128)S(1)}, s32[128]{0:T(128)}, u32[]{:S(2)}) copy-start(s32[128]{0:T(128)} %param.12) | copy-start | bytes 1540
  114.6 44.9 %all-to-all-start.1 = ((bf16[128,8,128]{2,0,1:T(8,128)(2,1)}), bf16[128,8,128]{2,0,1:T(8,128)(2,1)}, u32[]{:S(2)}, u32[]{:S(2)}) async-start(bf16[128,8,128]{2,0,1:T(8,128)(2,1)} %copy.25), calls=%async_computation.1 | async-start | bytes 524288 | tf_op jit(solution)/shard_map/all_to_all | solution.py:80
  150.4 1.9 %copy-start = (bf16[1024,1024]{1,0:T(8,128)(2,1)S(1)}, bf16[1024,1024]{1,0:T(8,128)(2,1)}, u32[]{:S(2)}) copy-start(bf16[1024,1024]{1,0:T(8,128)(2,1)} %all-gather.2.cloned.1.call-done) | copy-start | bytes 6291460
  152.3 3.2 %copy-start.1 = (bf16[4,256,1024]{2,1,0:T(8,128)(2,1)S(1)}, bf16[4,256,1024]{2,1,0:T(8,128)(2,1)}, u32[]{:S(2)}) copy-start(bf16[4,256,1024]{2,1,0:T(8,128)(2,1)} %copy.22) | copy-start | bytes 6291460
  152.3 3.2 %copy-start.7 = (bf16[128,1024]{0,1:T(8,128)(2,1)S(1)}, bf16[128,1024]{0,1:T(8,128)(2,1)}, u32[]{:S(2)}) copy-start(bf16[128,1024]{0,1:T(8,128)(2,1)} %get-tuple-element.6) | copy-start | bytes 786436
  152.3 3.2 %copy-start.8 = (bf16[128,1024]{0,1:T(8,128)(2,1)S(1)}, bf16[128,1024]{0,1:T(8,128)(2,1)}, u32[]{:S(2)}) copy-start(bf16[128,1024]{0,1:T(8,128)(2,1)} %get-tuple-element.7) | copy-start | bytes 786436
  153.6 23.0 %collective-permute-start.7 = (f32[256,512]{1,0:T(8,128)}, f32[256,512]{1,0:T(8,128)S(1)}, u32[]{:S(2)}, u32[]{:S(2)}) collective-permute-start(f32[256,512]{1,0:T(8,128)} %convolution_add_fusion), channel_id=1, source_target_pairs={{0,0},{1,8},{2,16},{3,24},{4,4},{5,12},{6,20},{7,28},{8,1},{9,9},{... | collective-permute-start | bytes 1572872 | tf_op jit(solution)/shard_map/ppermute | solution.py:106
Sparse Core Ops, SparseCore 0:
  59.9 34.1 all-reduce.1
Sparse Core Ops, SparseCore 1:
  70.8 47.7 all-gather.1
